TPU v7x, 256 devices: a whole 4x4x8 slice. The times are simulated.
256 devices in a mesh: ctx: 32 (over x, y, core), tp: 8 (over z).
Axes of the slice: x: 4, y: 4, z: 8, core: 2. Of those that a mesh axis runs over, the one named last changes fastest.
Arguments:
- hidden_states: bfloat16 [65536, 4096], P('ctx', 'tp')
- chosen: int32 [12288], P('ctx'), may hold values from 0 to 2048, as said below
- router_gate: float32 [12288], P('ctx'), may hold values from 0.2 to 1
- w_query: bfloat16 [4096, 4096], P(None, 'tp'), may hold values from -0.09375 to 0.09375
- w_key: bfloat16 [4096, 1024], P(None, 'tp'), may hold values from -0.09375 to 0.09375
- w_value: bfloat16 [4096, 1024], P(None, 'tp'), may hold values from -0.09375 to 0.09375
Outputs:
- attended: bfloat16 [12288, 4096], P('ctx', 'tp')
Inputs may be any that keep to these rules, and one draw needn't show every extreme that they name: `chosen`: each shard's 384 slots hold the sorted distinct positions of its routed tokens, then 2048 in every unused slot; a shard routes from 128 to 384 tokens, some shard exactly 384, and all shards together 65536 // 8.
All inputs are finite; a program needn't handle non-finite values.
Results may differ from a plain program's by a relative error of at most 0.035.
Values may be sent and summed in bfloat16 or wider, within the bound.
No kernel may reach another device: no remote copies, remote signals or barrier semaphores. Data moves between devices by JAX's collectives and lax.ppermute only.
A program may use at most 64 MiB of HBM per device.

v0:
```python
import math
import jax
import jax.numpy as jnp
from jax import lax
from jax.sharding import PartitionSpec as P

HEAD_DIM = 128
ROPE_BASE = 500000.0
MASKED = -1e30


def rotate(values_in, position):
    half_dim = values_in.shape[-1] // 2
    frequency = jnp.exp(
        jnp.arange(half_dim, dtype=jnp.float32) * (-2.0 * math.log(ROPE_BASE) / values_in.shape[-1])
    )
    angles = position.astype(jnp.float32)[:, None] * frequency[None, :]
    cosine = jnp.cos(angles)[:, None, :]
    sine = jnp.sin(angles)[:, None, :]
    first = values_in[..., :half_dim]
    second = values_in[..., half_dim:]
    return jnp.concatenate(
        [first * cosine - second * sine, second * cosine + first * sine], axis=-1
    )


def empty_state(count, kv_local, group, head_dim):
    return (
        jnp.full((kv_local, group, count), MASKED, jnp.float32),
        jnp.zeros((kv_local, group, count), jnp.float32),
        jnp.zeros((count, kv_local, group, head_dim), jnp.float32),
    )


def update(state, queries, query_pos, key_block, value_block, key_pos):
    running, totals, summed = state
    scores = jnp.einsum("rhgd,khd->hgrk", queries, key_block, preferred_element_type=jnp.float32)
    allowed = key_pos[None, None, None, :] <= query_pos[None, None, :, None]
    newest = jnp.maximum(running, jnp.max(jnp.where(allowed, scores, MASKED), axis=-1))
    factor = jnp.exp(running - newest)
    weights = jnp.where(allowed, jnp.exp(scores - newest[..., None]), 0.0)
    totals = totals * factor + jnp.sum(weights, axis=-1)
    mixed = jnp.einsum(
        "hgrk,khd->rhgd",
        weights.astype(jnp.bfloat16),
        value_block,
        preferred_element_type=jnp.float32,
    )
    summed = summed * jnp.transpose(factor, (2, 0, 1))[..., None] + mixed
    return (newest, totals, summed)


def finish(state):
    running, totals, summed = state
    denom = jnp.where(totals > 0.0, totals, 1.0)
    return summed / jnp.transpose(denom, (2, 0, 1))[..., None]


def highest(position, pad_mark):
    return jnp.max(jnp.where(position < pad_mark, position, -1))


def fold_keys(states, pieces, groups):
    key_rows, value_rows, key_pos = pieces
    length = key_rows.shape[0]
    block_rows = length
    for size_rows in (1536, 768, 384):
        block_rows = size_rows
        break
    blocks = length // block_rows
    shaped = (
        key_rows.reshape((blocks, block_rows) + key_rows.shape[1:]),
        value_rows.reshape((blocks, block_rows) + value_rows.shape[1:]),
        key_pos.reshape(blocks, block_rows),
    )

    def advance(carried, block):
        key_block, value_block, block_pos = block
        fresh = []
        for state, group_data in zip(carried, groups):
            queries, query_pos, limit = group_data

            def visit(current):
                return update(current, queries, query_pos, key_block, value_block, block_pos)

            def keep_state(current):
                return current

            fresh.append(lax.cond(jnp.min(block_pos) > limit, keep_state, visit, state))
        return (tuple(fresh), None)

    result, unused = lax.scan(advance, tuple(states), shaped)
    return result


def body(hidden_states, chosen, router_gate, w_query, w_key, w_value):
    seq_rows = hidden_states.shape[0]
    slot_count = chosen.shape[0]
    head_dim = HEAD_DIM
    query_width = w_query.shape[1]
    kv_width = w_key.shape[1]
    kv_local = kv_width // head_dim
    heads_local = query_width // head_dim
    group = heads_local // kv_local
    live = chosen < seq_rows
    pad_mark = lax.axis_size("ctx") * seq_rows + 1
    position = jnp.where(live, lax.axis_index("ctx") * seq_rows + chosen, pad_mark)
    picked = hidden_states[jnp.minimum(chosen, seq_rows - 1)]
    gated = jnp.where(live, router_gate, 0.0)
    piece = lax.all_gather(picked, "tp", axis=1, tiled=True)
    query_part = jnp.dot(piece, w_query, preferred_element_type=jnp.float32)
    key_part = jnp.dot(piece, w_key, preferred_element_type=jnp.float32)
    value_part = jnp.dot(piece, w_value, preferred_element_type=jnp.float32)
    queries = (
        rotate(query_part.reshape(slot_count, heads_local, head_dim), position) * head_dim ** (-0.5)
    ).astype(jnp.bfloat16)
    queries = queries.reshape(slot_count, kv_local, group, head_dim)
    key_rows = rotate(key_part.reshape(slot_count, kv_local, head_dim), position).astype(
        jnp.bfloat16
    )
    value_rows = value_part.reshape(slot_count, kv_local, head_dim).astype(jnp.bfloat16)
    groups = [(queries, position, highest(position, pad_mark))]
    states = fold_keys(
        (empty_state(slot_count, kv_local, group, head_dim),),
        (
            lax.all_gather(key_rows, "ctx", axis=0, tiled=True),
            lax.all_gather(value_rows, "ctx", axis=0, tiled=True),
            lax.all_gather(position, "ctx", axis=0, tiled=True),
        ),
        groups,
    )
    result = (finish(states[0]) * gated[:, None, None, None]).astype(jnp.bfloat16)
    return result.reshape(slot_count, query_width)


def solution(mesh):
    placed = (P("ctx", "tp"), P("ctx"), P("ctx"), P(None, "tp"), P(None, "tp"), P(None, "tp"))
    return jax.shard_map(
        body, mesh=mesh, in_specs=placed, out_specs=P("ctx", "tp"), check_vma=False
    )
```

profile of v0, /device:TPU:23, one launch (start us, length us, event | category | flops | bytes accessed | tf_op | source)
XLA Modules:
  0.0 253.6 jit_solution(8523070852562474726)
XLA Ops:
  6.5 0.8 fusion.37
  7.4 0.8 copy-done
  8.1 2.6 %gather_fusion = bf16[384,512]{1,0:T(8,128)(2,1)} fusion(bf16[2048,512]{1,0:T(8,128)(2,1)S(1)} %copy-done, s32[1024]{0:T(1024)S(1)} %pad_clamp_fusion), kind=kCustom, calls=%fused_computation | custom fusion | bytes 787968 | tf_op jit(solution)/shard_map/gather | solution.py:108
  10.8 47.3 %all-gather.9.cloned.1.call-done = bf16[384,4096]{1,0:T(8,128)(2,1)} async-done(((bf16[384,512]{1,0:T(8,128)(2,1)}), bf16[384,4096]{1,0:T(8,128)(2,1)}) %all-gather.9.cloned.1.call-update) | async-done | bytes 3145744 | tf_op jit(solution)/shard_map/all_gather | solution.py:110
  58.1 3.5 %convolution_convert_fusion = bf16[384,128]{1,0:T(8,128)(2,1)} fusion(bf16[384,4096]{1,0:T(8,128)(2,1)} %all-gather.9.cloned.1.call-done, bf16[4096,128]{1,0:T(8,128)(2,1)S(1)} %copy-done.1), kind=kOutput, calls=%fused_computation.29 | convolution fusion | flops 402702336 | bytes 4292608 | tf_op jit(solution)/shard_map/dot_general | solution.py:113
  61.6 3.2 %convolution_bitcast_fusion = f32[384,1,128]{0,2,1:T(8,128)S(1)} fusion(bf16[384,4096]{1,0:T(8,128)(2,1)} %all-gather.9.cloned.1.call-done, bf16[4096,128]{1,0:T(8,128)(2,1)} %param.14), kind=kOutput, calls=%fused_computation.28 | convolution fusion | flops 402653184 | bytes 4390912 | tf_op jit(solution)/shard_map/dot_general | solution.py:112
  64.8 0.4 fusion.31
  65.3 0.7 pad_maximum_fusion
  66.0 23.6 %all-gather.2 = s32[32,1,384]{2,1,0:T(1,128)S(1)} all-gather(s32[1,1,384]{2,1,0:T(1,128)S(1)} %reshape.287), channel_id=1, replica_groups=mesh['ctx'=32,'tp'=8] {'ctx'}, dimensions={0}, use_global_device_ids=true | all-gather | bytes 50688 | tf_op jit(solution)/shard_map/all_gather | solution.py:128
  89.7 0.7 fusion.35
  90.4 0.8 multiply_cosine_fusion
  91.2 5.8 %fusion.39 = f32[384,512]{1,0:T(8,128)} fusion(bf16[384,4096]{1,0:T(8,128)(2,1)} %all-gather.9.cloned.1.call-done, bf16[4096,512]{1,0:T(8,128)(2,1)} %param.13), kind=kOutput, calls=%fused_computation.61 | convolution fusion | flops 1610612736 | bytes 8126464 | tf_op jit(solution)/shard_map/dot_general | solution.py:111
  97.0 1.4 reshape.272
  98.4 0.5 fusion.38
  99.3 10.0 %all-gather.11.cloned.1.call-done = bf16[12288,128]{1,0:T(8,128)(2,1)} async-done(((bf16[384,128]{1,0:T(8,128)(2,1)}), bf16[12288,128]{1,0:T(8,128)(2,1)}) %all-gather.11.cloned.1.call-update) | async-done | bytes 3145744 | tf_op jit(solution)/shard_map/all_gather | solution.py:127
  109.3 4.6 %copy.17 = bf16[8,1536,1,128]{1,3,2,0:T(8,128)(2,1)} copy(bf16[8,1536,1,128]{3,1,0,2:T(8,128)(2,1)} %bitcast.82) | data formatting | bytes 6291456 | tf_op jit(solution)/shard_map/while | solution.py:92
  113.9 48.9 %all-gather.7.cloned.1.call-done = bf16[12288,1,128]{0,2,1:T(8,128)(2,1)} async-done(((bf16[384,1,128]{0,2,1:T(8,128)(2,1)}), bf16[12288,1,128]{0,2,1:T(8,128)(2,1)}) %all-gather.7.cloned.1.call-update) | async-done | bytes 3145744 | tf_op jit(solution)/shard_map/all_gather | solution.py:126
  162.8 4.6 %copy.20 = bf16[12288,1,128]{2,0,1:T(8,128)(2,1)} copy(bf16[12288,1,128]{0,2,1:T(8,128)(2,1)} %all-gather.7.cloned.1.call-done) | data formatting | bytes 6291456 | tf_op jit(solution)/shard_map/while | solution.py:92
  167.5 78.5 %while.14 = (s32[]{:T(128)}, f32[1,4,384]{2,1,0:T(4,128)S(1)}, f32[1,4,384]{2,1,0:T(4,128)S(1)}, f32[384,1,4,128]{0,3,2,1:T(8,128)S(1)}, s32[8,1536]{1,0:T(8,128...) while((s32[]{:T(128)}, f32[1,4,384]{2,1,0:T(4,128)S(1)}, ...), condition=%wide.region_7.8_spmd, body=%wide.region_1.7_spmd.sunk | while | flops 1227823104 | bytes 33555200 | solution.py:92
  167.6 0.7 fusion.47
  169.5 7.9 %conditional.2 = (f32[1,4,384]{2,1,0:T(4,128)S(1)}, f32[1,4,384]{2,1,0:T(4,128)S(1)}, f32[384,1,4,128]{0,3,2,1:T(8,128)S(1)}) conditional(s32[]{:T(128)} %convert_element_type.58, (s32[1,1536]{1,0:T(1,128)S(1)}, s32[384]{0:T(512)S(1)}, bf16[8,1536,1,128]{3,1,2,0:T(8,128)(2,1)}, s32[]{:T(128)}, bf16[384,1,4,128]{3,0,2,1:T(8,128)(2,1)S(1)}, ...), branch_computations={%region_3.5_spmd, %region_6.6_spmd} | conditional | flops 1227821568 | bytes 33530396 | solution.py:89
  169.5 0.4 broadcast_compare_fusion
  169.9 2.5 fusion
  172.4 1.7 fusion.4
  174.2 3.2 %fusion.12 = f32[384,1,4,128]{0,3,2,1:T(8,128)S(1)} fusion(f32[1536,384,4]{1,0,2:T(8,128)S(1)} %get-tuple-element.191, f32[4,384]{1,0:T(4,128)S(1)} %bitcast.84, pred[384,1536]{0,1:T(8,128)(4,1)S(1)} %broadcast_compare_fusion, f32[384,1,4,128]{0,3,2,1:T(8,128)S(1)} %get-tuple-element.124, bf16[8,1536,1,128]{1,3,2,0:T(8,128)(2,1)} %get-tuple-element.125, ...), kind=kOutput, calls=%fused_computation.12 | convolution fusion | flops 611450880 | bytes 12005888 | tf_op jit(solution)/shard_map/while/body/eval_jaxpr/cond/branch_0_fun/hgrk,khd->rhgd/dot_general | solution.py:43
  177.4 0.7 fusion.47
  179.3 7.9 %conditional.2 = (f32[1,4,384]{2,1,0:T(4,128)S(1)}, f32[1,4,384]{2,1,0:T(4,128)S(1)}, f32[384,1,4,128]{0,3,2,1:T(8,128)S(1)}) conditional(s32[]{:T(128)} %convert_element_type.58, (s32[1,1536]{1,0:T(1,128)S(1)}, s32[384]{0:T(512)S(1)}, bf16[8,1536,1,128]{3,1,2,0:T(8,128)(2,1)}, s32[]{:T(128)}, bf16[384,1,4,128]{3,0,2,1:T(8,128)(2,1)S(1)}, ...), branch_computations={%region_3.5_spmd, %region_6.6_spmd} | conditional | flops 1227821568 | bytes 33530396 | solution.py:89
  179.3 0.4 broadcast_compare_fusion
  179.7 2.5 fusion
  182.2 1.7 fusion.4
  184.0 3.2 %fusion.12 = f32[384,1,4,128]{0,3,2,1:T(8,128)S(1)} fusion(f32[1536,384,4]{1,0,2:T(8,128)S(1)} %get-tuple-element.191, f32[4,384]{1,0:T(4,128)S(1)} %bitcast.84, pred[384,1536]{0,1:T(8,128)(4,1)S(1)} %broadcast_compare_fusion, f32[384,1,4,128]{0,3,2,1:T(8,128)S(1)} %get-tuple-element.124, bf16[8,1536,1,128]{1,3,2,0:T(8,128)(2,1)} %get-tuple-element.125, ...), kind=kOutput, calls=%fused_computation.12 | convolution fusion | flops 611450880 | bytes 12005888 | tf_op jit(solution)/shard_map/while/body/eval_jaxpr/cond/branch_0_fun/hgrk,khd->rhgd/dot_general | solution.py:43
  187.2 0.7 fusion.47
  189.1 7.9 %conditional.2 = (f32[1,4,384]{2,1,0:T(4,128)S(1)}, f32[1,4,384]{2,1,0:T(4,128)S(1)}, f32[384,1,4,128]{0,3,2,1:T(8,128)S(1)}) conditional(s32[]{:T(128)} %convert_element_type.58, (s32[1,1536]{1,0:T(1,128)S(1)}, s32[384]{0:T(512)S(1)}, bf16[8,1536,1,128]{3,1,2,0:T(8,128)(2,1)}, s32[]{:T(128)}, bf16[384,1,4,128]{3,0,2,1:T(8,128)(2,1)S(1)}, ...), branch_computations={%region_3.5_spmd, %region_6.6_spmd} | conditional | flops 1227821568 | bytes 33530396 | solution.py:89
  189.5 2.5 fusion
  192.1 1.7 fusion.4
  193.8 3.2 %fusion.12 = f32[384,1,4,128]{0,3,2,1:T(8,128)S(1)} fusion(f32[1536,384,4]{1,0,2:T(8,128)S(1)} %get-tuple-element.191, f32[4,384]{1,0:T(4,128)S(1)} %bitcast.84, pred[384,1536]{0,1:T(8,128)(4,1)S(1)} %broadcast_compare_fusion, f32[384,1,4,128]{0,3,2,1:T(8,128)S(1)} %get-tuple-element.124, bf16[8,1536,1,128]{1,3,2,0:T(8,128)(2,1)} %get-tuple-element.125, ...), kind=kOutput, calls=%fused_computation.12 | convolution fusion | flops 611450880 | bytes 12005888 | tf_op jit(solution)/shard_map/while/body/eval_jaxpr/cond/branch_0_fun/hgrk,khd->rhgd/dot_general | solution.py:43
  197.0 0.7 fusion.47
  198.9 7.9 %conditional.2 = (f32[1,4,384]{2,1,0:T(4,128)S(1)}, f32[1,4,384]{2,1,0:T(4,128)S(1)}, f32[384,1,4,128]{0,3,2,1:T(8,128)S(1)}) conditional(s32[]{:T(128)} %convert_element_type.58, (s32[1,1536]{1,0:T(1,128)S(1)}, s32[384]{0:T(512)S(1)}, bf16[8,1536,1,128]{3,1,2,0:T(8,128)(2,1)}, s32[]{:T(128)}, bf16[384,1,4,128]{3,0,2,1:T(8,128)(2,1)S(1)}, ...), branch_computations={%region_3.5_spmd, %region_6.6_spmd} | conditional | flops 1227821568 | bytes 33530396 | solution.py:89
  199.3 2.5 fusion
  201.9 1.7 fusion.4
  203.6 3.2 %fusion.12 = f32[384,1,4,128]{0,3,2,1:T(8,128)S(1)} fusion(f32[1536,384,4]{1,0,2:T(8,128)S(1)} %get-tuple-element.191, f32[4,384]{1,0:T(4,128)S(1)} %bitcast.84, pred[384,1536]{0,1:T(8,128)(4,1)S(1)} %broadcast_compare_fusion, f32[384,1,4,128]{0,3,2,1:T(8,128)S(1)} %get-tuple-element.124, bf16[8,1536,1,128]{1,3,2,0:T(8,128)(2,1)} %get-tuple-element.125, ...), kind=kOutput, calls=%fused_computation.12 | convolution fusion | flops 611450880 | bytes 12005888 | tf_op jit(solution)/shard_map/while/body/eval_jaxpr/cond/branch_0_fun/hgrk,khd->rhgd/dot_general | solution.py:43
  206.8 0.7 fusion.47
  208.7 7.9 %conditional.2 = (f32[1,4,384]{2,1,0:T(4,128)S(1)}, f32[1,4,384]{2,1,0:T(4,128)S(1)}, f32[384,1,4,128]{0,3,2,1:T(8,128)S(1)}) conditional(s32[]{:T(128)} %convert_element_type.58, (s32[1,1536]{1,0:T(1,128)S(1)}, s32[384]{0:T(512)S(1)}, bf16[8,1536,1,128]{3,1,2,0:T(8,128)(2,1)}, s32[]{:T(128)}, bf16[384,1,4,128]{3,0,2,1:T(8,128)(2,1)S(1)}, ...), branch_computations={%region_3.5_spmd, %region_6.6_spmd} | conditional | flops 1227821568 | bytes 33530396 | solution.py:89
  208.8 0.4 broadcast_compare_fusion
  209.2 2.5 fusion
  211.7 1.7 fusion.4
  213.4 3.2 %fusion.12 = f32[384,1,4,128]{0,3,2,1:T(8,128)S(1)} fusion(f32[1536,384,4]{1,0,2:T(8,128)S(1)} %get-tuple-element.191, f32[4,384]{1,0:T(4,128)S(1)} %bitcast.84, pred[384,1536]{0,1:T(8,128)(4,1)S(1)} %broadcast_compare_fusion, f32[384,1,4,128]{0,3,2,1:T(8,128)S(1)} %get-tuple-element.124, bf16[8,1536,1,128]{1,3,2,0:T(8,128)(2,1)} %get-tuple-element.125, ...), kind=kOutput, calls=%fused_computation.12 | convolution fusion | flops 611450880 | bytes 12005888 | tf_op jit(solution)/shard_map/while/body/eval_jaxpr/cond/branch_0_fun/hgrk,khd->rhgd/dot_general | solution.py:43
  216.6 0.7 fusion.47
  218.5 7.9 %conditional.2 = (f32[1,4,384]{2,1,0:T(4,128)S(1)}, f32[1,4,384]{2,1,0:T(4,128)S(1)}, f32[384,1,4,128]{0,3,2,1:T(8,128)S(1)}) conditional(s32[]{:T(128)} %convert_element_type.58, (s32[1,1536]{1,0:T(1,128)S(1)}, s32[384]{0:T(512)S(1)}, bf16[8,1536,1,128]{3,1,2,0:T(8,128)(2,1)}, s32[]{:T(128)}, bf16[384,1,4,128]{3,0,2,1:T(8,128)(2,1)S(1)}, ...), branch_computations={%region_3.5_spmd, %region_6.6_spmd} | conditional | flops 1227821568 | bytes 33530396 | solution.py:89
  219.0 2.5 fusion
  221.5 1.7 fusion.4
  223.2 3.2 %fusion.12 = f32[384,1,4,128]{0,3,2,1:T(8,128)S(1)} fusion(f32[1536,384,4]{1,0,2:T(8,128)S(1)} %get-tuple-element.191, f32[4,384]{1,0:T(4,128)S(1)} %bitcast.84, pred[384,1536]{0,1:T(8,128)(4,1)S(1)} %broadcast_compare_fusion, f32[384,1,4,128]{0,3,2,1:T(8,128)S(1)} %get-tuple-element.124, bf16[8,1536,1,128]{1,3,2,0:T(8,128)(2,1)} %get-tuple-element.125, ...), kind=kOutput, calls=%fused_computation.12 | convolution fusion | flops 611450880 | bytes 12005888 | tf_op jit(solution)/shard_map/while/body/eval_jaxpr/cond/branch_0_fun/hgrk,khd->rhgd/dot_general | solution.py:43
  226.4 0.7 fusion.47
  228.3 7.9 %conditional.2 = (f32[1,4,384]{2,1,0:T(4,128)S(1)}, f32[1,4,384]{2,1,0:T(4,128)S(1)}, f32[384,1,4,128]{0,3,2,1:T(8,128)S(1)}) conditional(s32[]{:T(128)} %convert_element_type.58, (s32[1,1536]{1,0:T(1,128)S(1)}, s32[384]{0:T(512)S(1)}, bf16[8,1536,1,128]{3,1,2,0:T(8,128)(2,1)}, s32[]{:T(128)}, bf16[384,1,4,128]{3,0,2,1:T(8,128)(2,1)S(1)}, ...), branch_computations={%region_3.5_spmd, %region_6.6_spmd} | conditional | flops 1227821568 | bytes 33530396 | solution.py:89
  228.8 2.5 fusion
  231.3 1.7 fusion.4
  233.0 3.2 %fusion.12 = f32[384,1,4,128]{0,3,2,1:T(8,128)S(1)} fusion(f32[1536,384,4]{1,0,2:T(8,128)S(1)} %get-tuple-element.191, f32[4,384]{1,0:T(4,128)S(1)} %bitcast.84, pred[384,1536]{0,1:T(8,128)(4,1)S(1)} %broadcast_compare_fusion, f32[384,1,4,128]{0,3,2,1:T(8,128)S(1)} %get-tuple-element.124, bf16[8,1536,1,128]{1,3,2,0:T(8,128)(2,1)} %get-tuple-element.125, ...), kind=kOutput, calls=%fused_computation.12 | convolution fusion | flops 611450880 | bytes 12005888 | tf_op jit(solution)/shard_map/while/body/eval_jaxpr/cond/branch_0_fun/hgrk,khd->rhgd/dot_general | solution.py:43
  236.2 0.7 fusion.47
  238.2 7.9 %conditional.2 = (f32[1,4,384]{2,1,0:T(4,128)S(1)}, f32[1,4,384]{2,1,0:T(4,128)S(1)}, f32[384,1,4,128]{0,3,2,1:T(8,128)S(1)}) conditional(s32[]{:T(128)} %convert_element_type.58, (s32[1,1536]{1,0:T(1,128)S(1)}, s32[384]{0:T(512)S(1)}, bf16[8,1536,1,128]{3,1,2,0:T(8,128)(2,1)}, s32[]{:T(128)}, bf16[384,1,4,128]{3,0,2,1:T(8,128)(2,1)S(1)}, ...), branch_computations={%region_3.5_spmd, %region_6.6_spmd} | conditional | flops 1227821568 | bytes 33530396 | solution.py:89
  238.2 0.4 broadcast_compare_fusion
  238.6 2.5 fusion
  241.1 1.7 fusion.4
  242.8 3.2 %fusion.12 = f32[384,1,4,128]{0,3,2,1:T(8,128)S(1)} fusion(f32[1536,384,4]{1,0,2:T(8,128)S(1)} %get-tuple-element.191, f32[4,384]{1,0:T(4,128)S(1)} %bitcast.84, pred[384,1536]{0,1:T(8,128)(4,1)S(1)} %broadcast_compare_fusion, f32[384,1,4,128]{0,3,2,1:T(8,128)S(1)} %get-tuple-element.124, bf16[8,1536,1,128]{1,3,2,0:T(8,128)(2,1)} %get-tuple-element.125, ...), kind=kOutput, calls=%fused_computation.12 | convolution fusion | flops 611450880 | bytes 12005888 | tf_op jit(solution)/shard_map/while/body/eval_jaxpr/cond/branch_0_fun/hgrk,khd->rhgd/dot_general | solution.py:43
  246.1 0.9 copy.21
  (62 shorter events, 2.9 us)
Async XLA Ops:
  6.5 1.6 copy-start
  6.5 51.5 %copy-start.1 = (bf16[4096,128]{1,0:T(8,128)(2,1)S(1)}, bf16[4096,128]{1,0:T(8,128)(2,1)}, u32[]{:S(2)}) copy-start(bf16[4096,128]{1,0:T(8,128)(2,1)} %param.15) | copy-start | bytes 3145732
  6.5 51.5 %all-gather.9.cloned.1.call-start = ((), (), s32[]{:S(2)}) async-start(), calls=%async_computation.1 | async-start | bytes 3538944 | tf_op jit(solution)/shard_map/all_gather | solution.py:110
  10.7 98.6 %all-gather.11.cloned.1.call-start = ((), (), s32[]{:S(2)}) async-start(), calls=%async_computation.2 | async-start | bytes 3244032 | tf_op jit(solution)/shard_map/all_gather | solution.py:127
  61.6 28.9 %copy-start.2 = (s32[384]{0:T(512)S(1)}, s32[384]{0:T(512)}, u32[]{:S(2)}) copy-start(s32[384]{0:T(512)} %param.11) | copy-start | bytes 4612
  61.6 28.9 %copy-start.3 = (f32[384]{0:T(512)S(1)}, f32[384]{0:T(512)}, u32[]{:S(2)}) copy-start(f32[384]{0:T(512)} %param.12) | copy-start | bytes 4612
  61.6 101.2 %all-gather.7.cloned.1.call-start = ((), (), s32[]{:S(2)}) async-start(), calls=%async_computation | async-start | bytes 3244032 | tf_op jit(solution)/shard_map/all_gather | solution.py:126
Sparse Core Ops, SparseCore 0:
  10.9 47.1 all-gather.8
  61.7 47.5 all-gather.10
  111.8 51.0 all-gather.6
where the time goes:
time: 255 us; the launch traced here: 254 us
  waiting for transfers between devices  106 us (42%)
  matrix products  57.8 us (23%)
  other arithmetic  26.3 us (10%)
  blocking collectives  23.6 us (9%)
  local copies, waits for them, and re-layouts  15.5 us (6%)
  between operations  13.2 us (5%)
  loops' own time  10.8 us (4%)
    all_gather x1, waiting for transfers between devices, body(): lax.all_gather(key_rows, 'ctx', axis=0, tiled=True)  48.9 us
    all_gather x1, waiting for transfers between devices, body(): piece = lax.all_gather(picked, 'tp', axis=1, tiled=True)  47.3 us
    dot_general x8, matrix products, update(): jnp.einsum('hgrk,khd->rhgd', weights.astype(jnp.bfloat16), value_block, p...  25.3 us
    all_gather x1, blocking collectives, body(): lax.all_gather(position, 'ctx', axis=0, tiled=True)  23.6 us
    dot_general x8, matrix products, update(): jnp.einsum('rhgd,khd->hgrk', queries, key_block, preferred_element_type=j...  20.1 us
    reduce_sum x8, other arithmetic, update(): totals = totals * factor + jnp.sum(weights, axis=-1)  13.6 us
    another operation x1, loops' own time, fold_keys(): result, unused = lax.scan(advance, tuple(states), shaped)  10.4 us
    all_gather x1, waiting for transfers between devices, body(): lax.all_gather(value_rows, 'ctx', axis=0, tiled=True)  9.97 us
  transfers between devices with their start and end apart: 3, of which 3 were waited for; matrix products, arithmetic and copies ran while one was open for 7% of the time, Pallas kernels for 0%

commit v1 on v0

--- a/solution.py
+++ b/solution.py
@@ -107,7 +107,15 @@
     position = jnp.where(live, lax.axis_index("ctx") * seq_rows + chosen, pad_mark)
     picked = hidden_states[jnp.minimum(chosen, seq_rows - 1)]
     gated = jnp.where(live, router_gate, 0.0)
-    piece = lax.all_gather(picked, "tp", axis=1, tiled=True)
+    piece = jnp.concatenate(
+        lax.all_to_all(
+            jnp.stack([picked for _ in range(lax.psum(1, "tp"))]),
+            split_axis=0,
+            concat_axis=0,
+            axis_name="tp",
+        ),
+        1,
+    )
     query_part = jnp.dot(piece, w_query, preferred_element_type=jnp.float32)
     key_part = jnp.dot(piece, w_key, preferred_element_type=jnp.float32)
     value_part = jnp.dot(piece, w_value, preferred_element_type=jnp.float32)

time: 255 us -> 288 us (1.13)
  blocking collectives: 23.6 us -> 105 us
  waiting for transfers between devices: 106 us -> 41.4 us
  local copies, waits for them, and re-layouts: 15.5 us -> 34.7 us
    all_to_all x0 -> x1, blocking collectives: none -> 80.3 us  [body(): lax.all_to_all(jnp.stack([picked for _ in range(lax.psum(1, 'tp'))]), spl...]
    all_gather x1 -> x0, waiting for transfers between devices: 47.3 us -> none  [body(): piece = lax.all_gather(picked, 'tp', axis=1, tiled=True)]
    reshape x1 -> x3, local copies, waits for them, and re-layouts: 1.39 us -> 11.7 us  [body(): jnp.concatenate(lax.all_to_all(jnp.stack([picked for _ in range(lax.psum(...]
    all_gather x1, waiting for transfers between devices: 9.97 us -> 0.02 us  [body(): lax.all_gather(value_rows, 'ctx', axis=0, tiled=True)]
    all_gather x1, waiting for transfers between devices: 48.9 us -> 41.3 us  [body(): lax.all_gather(key_rows, 'ctx', axis=0, tiled=True)]
    dot_general x0 -> x1, local copies, waits for them, and re-layouts: none -> 6.45 us  [body(): query_part = jnp.dot(piece, w_query, preferred_element_type=jnp.float32)]
    unnamed x9 -> x15, local copies, waits for them, and re-layouts: 0.77 us -> 3.73 us
    while x2 -> x3, local copies, waits for them, and re-layouts: 9.28 us -> 9.52 us  [fold_keys(): result, unused = lax.scan(advance, tuple(states), shaped)]
  transfers between devices with their start and end apart: 3 -> 2, of which waited for: 3 -> 1; matrix products, arithmetic and copies ran while one was open for 7% -> 12% of each run, Pallas kernels for 0% -> 0%
where the time goes in v1:
time: 288 us; the launch traced here: 287 us
  blocking collectives  105 us (36%)
  matrix products  55.3 us (19%)
  waiting for transfers between devices  41.4 us (14%)
  local copies, waits for them, and re-layouts  34.7 us (12%)
  other arithmetic  25.7 us (9%)
  between operations  13.6 us (5%)
  loops' own time  10.9 us (4%)
    all_to_all x1, blocking collectives, body(): lax.all_to_all(jnp.stack([picked for _ in range(lax.psum(1, 'tp'))]), spl...  80.3 us
    all_gather x1, waiting for transfers between devices, body(): lax.all_gather(key_rows, 'ctx', axis=0, tiled=True)  41.3 us
    dot_general x8, matrix products, update(): jnp.einsum('hgrk,khd->rhgd', weights.astype(jnp.bfloat16), value_block, p...  25.2 us
    all_gather x1, blocking collectives, body(): lax.all_gather(position, 'ctx', axis=0, tiled=True)  24.8 us
    dot_general x8, matrix products, update(): jnp.einsum('rhgd,khd->hgrk', queries, key_block, preferred_element_type=j...  20.1 us
    reduce_sum x8, other arithmetic, update(): totals = totals * factor + jnp.sum(weights, axis=-1)  13.6 us
    reshape x3, local copies, waits for them, and re-layouts, body(): jnp.concatenate(lax.all_to_all(jnp.stack([picked for _ in range(lax.psum(...  11.7 us
    another operation x1, loops' own time, fold_keys(): result, unused = lax.scan(advance, tuple(states), shaped)  10.5 us
  transfers between devices with their start and end apart: 2, of which 1 were waited for; matrix products, arithmetic and copies ran while one was open for 12% of the time, Pallas kernels for 0%

profile of v1, /device:TPU:23, one launch (start us, length us, event | category | flops | bytes accessed | tf_op | source)
XLA Modules:
  0.0 286.8 jit_solution(10068599358649758571)
XLA Ops:
  6.5 0.8 fusion.37
  7.4 0.8 copy-done
  8.1 2.1 gather_fusion
  10.5 80.3 %all_to_all.5 = bf16[8,384,512]{2,1,0:T(8,128)(2,1)S(1)} all-to-all(bf16[8,384,512]{2,1,0:T(8,128)(2,1)S(1)} %stack.2), channel_id=1, replica_groups=mesh['ctx'=32,'tp'=8] {'tp'}, dimensions={0} | all-to-all | bytes 6291456 | tf_op jit(solution)/shard_map/all_to_all | solution.py:111
  90.8 0.4 copy.24
  91.2 1.3 copy-done.1
  92.5 1.6 copy-done.2
  94.1 1.6 convolution_convert_fusion
  95.9 2.9 %convolution_bitcast_fusion = f32[384,1,128]{0,2,1:T(8,128)S(1)} fusion(bf16[384,4096]{1,0:T(8,128)(2,1)} %bitcast.89, bf16[4096,128]{1,0:T(8,128)(2,1)S(1)} %copy-done.4), kind=kOutput, calls=%fused_computation.28 | convolution fusion | flops 402653184 | bytes 4390912 | tf_op jit(solution)/shard_map/dot_general | solution.py:120
  98.8 0.4 fusion.31
  99.2 0.7 pad_maximum_fusion
  99.9 6.4 %copy.22 = bf16[512,4096]{1,0:T(8,128)(2,1)} copy(bf16[512,4096]{0,1:T(8,128)(2,1)} %bitcast.91) | data formatting | bytes 8388608 | tf_op jit(solution)/shard_map/dot_general | solution.py:119
  106.4 24.8 %all-gather.1 = s32[32,1,384]{2,1,0:T(1,128)S(1)} all-gather(s32[1,1,384]{2,1,0:T(1,128)S(1)} %reshape.294), channel_id=1, replica_groups=mesh['ctx'=32,'tp'=8] {'ctx'}, dimensions={0}, use_global_device_ids=true | all-gather | bytes 50688 | tf_op jit(solution)/shard_map/all_gather | solution.py:136
  131.3 0.7 fusion.35
  132.0 0.4 multiply_cosine_fusion
  132.4 5.4 %copy.14 = bf16[384,8,512]{2,1,0:T(8,128)(2,1)} copy(bf16[384,8,512]{2,0,1:T(8,128)(2,1)} %bitcast.87) | data formatting | bytes 6291456 | tf_op jit(solution)/shard_map/reshape | solution.py:110
  137.8 5.9 %reshape.299 = bf16[384,4096,1]{1,0,2:T(8,128)(2,1)} reshape(bf16[384,8,512]{2,1,0:T(8,128)(2,1)} %copy.14) | data formatting | bytes 6291456 | tf_op jit(solution)/shard_map/reshape | solution.py:110
  143.7 5.5 %fusion.38 = f32[384,4,128]{0,2,1:T(8,128)S(1)} fusion(bf16[384,4096,1]{1,0,2:T(8,128)(2,1)} %reshape.299, bf16[4,128,4096]{2,1,0:T(8,128)(2,1)} %bitcast.92), kind=kOutput, calls=%fused_computation.60 | convolution fusion | flops 1610612736 | bytes 8126464 | tf_op jit(solution)/shard_map/dot_general | solution.py:119
  149.6 4.7 %copy.18 = bf16[8,1536,1,128]{1,3,2,0:T(8,128)(2,1)} copy(bf16[8,1536,1,128]{3,1,0,2:T(8,128)(2,1)} %bitcast.93) | data formatting | bytes 6291456 | tf_op jit(solution)/shard_map/while | solution.py:92
  154.3 41.3 %all-gather.5.cloned.1.call-done = bf16[12288,1,128]{0,2,1:T(8,128)(2,1)} async-done(((bf16[384,1,128]{0,2,1:T(8,128)(2,1)}), bf16[12288,1,128]{0,2,1:T(8,128)(2,1)}) %all-gather.5.cloned.1.call-update) | async-done | bytes 3145744 | tf_op jit(solution)/shard_map/all_gather | solution.py:134
  195.6 4.6 %copy.21 = bf16[12288,1,128]{2,0,1:T(8,128)(2,1)} copy(bf16[12288,1,128]{0,2,1:T(8,128)(2,1)} %all-gather.5.cloned.1.call-done) | data formatting | bytes 6291456 | tf_op jit(solution)/shard_map/while | solution.py:92
  200.3 78.6 %while.14 = (s32[]{:T(128)}, f32[1,4,384]{2,1,0:T(4,128)S(1)}, f32[1,4,384]{2,1,0:T(4,128)S(1)}, f32[384,1,4,128]{0,3,2,1:T(8,128)S(1)}, s32[8,1536]{1,0:T(8,128...) while((s32[]{:T(128)}, f32[1,4,384]{2,1,0:T(4,128)S(1)}, ...), condition=%wide.region_7.8_spmd, body=%wide.region_1.7_spmd.sunk | while | flops 1227823104 | bytes 33555200 | solution.py:92
  200.3 0.7 fusion.46
  202.3 7.9 %conditional.2 = (f32[1,4,384]{2,1,0:T(4,128)S(1)}, f32[1,4,384]{2,1,0:T(4,128)S(1)}, f32[384,1,4,128]{0,3,2,1:T(8,128)S(1)}) conditional(s32[]{:T(128)} %convert_element_type.58, (s32[1,1536]{1,0:T(1,128)S(1)}, s32[384]{0:T(512)S(1)}, bf16[8,1536,1,128]{3,1,2,0:T(8,128)(2,1)}, s32[]{:T(128)}, bf16[384,1,4,128]{3,0,2,1:T(8,128)(2,1)S(1)}, ...), branch_computations={%region_3.5_spmd, %region_6.6_spmd} | conditional | flops 1227821568 | bytes 33530396 | solution.py:89
  202.7 2.5 fusion
  205.2 1.7 fusion.4
  206.9 3.2 %fusion.12 = f32[384,1,4,128]{0,3,2,1:T(8,128)S(1)} fusion(f32[1536,384,4]{1,0,2:T(8,128)S(1)} %get-tuple-element.191, f32[4,384]{1,0:T(4,128)S(1)} %bitcast.95, pred[384,1536]{0,1:T(8,128)(4,1)S(1)} %broadcast_compare_fusion, f32[384,1,4,128]{0,3,2,1:T(8,128)S(1)} %get-tuple-element.124, bf16[8,1536,1,128]{1,3,2,0:T(8,128)(2,1)} %get-tuple-element.125, ...), kind=kOutput, calls=%fused_computation.12 | convolution fusion | flops 611450880 | bytes 12005888 | tf_op jit(solution)/shard_map/while/body/eval_jaxpr/cond/branch_0_fun/hgrk,khd->rhgd/dot_general | solution.py:43
  210.2 0.7 fusion.46
  212.1 7.9 %conditional.2 = (f32[1,4,384]{2,1,0:T(4,128)S(1)}, f32[1,4,384]{2,1,0:T(4,128)S(1)}, f32[384,1,4,128]{0,3,2,1:T(8,128)S(1)}) conditional(s32[]{:T(128)} %convert_element_type.58, (s32[1,1536]{1,0:T(1,128)S(1)}, s32[384]{0:T(512)S(1)}, bf16[8,1536,1,128]{3,1,2,0:T(8,128)(2,1)}, s32[]{:T(128)}, bf16[384,1,4,128]{3,0,2,1:T(8,128)(2,1)S(1)}, ...), branch_computations={%region_3.5_spmd, %region_6.6_spmd} | conditional | flops 1227821568 | bytes 33530396 | solution.py:89
  212.5 2.5 fusion
  215.0 1.7 fusion.4
  216.8 3.2 %fusion.12 = f32[384,1,4,128]{0,3,2,1:T(8,128)S(1)} fusion(f32[1536,384,4]{1,0,2:T(8,128)S(1)} %get-tuple-element.191, f32[4,384]{1,0:T(4,128)S(1)} %bitcast.95, pred[384,1536]{0,1:T(8,128)(4,1)S(1)} %broadcast_compare_fusion, f32[384,1,4,128]{0,3,2,1:T(8,128)S(1)} %get-tuple-element.124, bf16[8,1536,1,128]{1,3,2,0:T(8,128)(2,1)} %get-tuple-element.125, ...), kind=kOutput, calls=%fused_computation.12 | convolution fusion | flops 611450880 | bytes 12005888 | tf_op jit(solution)/shard_map/while/body/eval_jaxpr/cond/branch_0_fun/hgrk,khd->rhgd/dot_general | solution.py:43
  220.0 0.7 fusion.46
  221.9 7.9 %conditional.2 = (f32[1,4,384]{2,1,0:T(4,128)S(1)}, f32[1,4,384]{2,1,0:T(4,128)S(1)}, f32[384,1,4,128]{0,3,2,1:T(8,128)S(1)}) conditional(s32[]{:T(128)} %convert_element_type.58, (s32[1,1536]{1,0:T(1,128)S(1)}, s32[384]{0:T(512)S(1)}, bf16[8,1536,1,128]{3,1,2,0:T(8,128)(2,1)}, s32[]{:T(128)}, bf16[384,1,4,128]{3,0,2,1:T(8,128)(2,1)S(1)}, ...), branch_computations={%region_3.5_spmd, %region_6.6_spmd} | conditional | flops 1227821568 | bytes 33530396 | solution.py:89
  222.3 2.5 fusion
  224.9 1.7 fusion.4
  226.6 3.2 %fusion.12 = f32[384,1,4,128]{0,3,2,1:T(8,128)S(1)} fusion(f32[1536,384,4]{1,0,2:T(8,128)S(1)} %get-tuple-element.191, f32[4,384]{1,0:T(4,128)S(1)} %bitcast.95, pred[384,1536]{0,1:T(8,128)(4,1)S(1)} %broadcast_compare_fusion, f32[384,1,4,128]{0,3,2,1:T(8,128)S(1)} %get-tuple-element.124, bf16[8,1536,1,128]{1,3,2,0:T(8,128)(2,1)} %get-tuple-element.125, ...), kind=kOutput, calls=%fused_computation.12 | convolution fusion | flops 611450880 | bytes 12005888 | tf_op jit(solution)/shard_map/while/body/eval_jaxpr/cond/branch_0_fun/hgrk,khd->rhgd/dot_general | solution.py:43
  229.8 0.7 fusion.46
  231.7 7.9 %conditional.2 = (f32[1,4,384]{2,1,0:T(4,128)S(1)}, f32[1,4,384]{2,1,0:T(4,128)S(1)}, f32[384,1,4,128]{0,3,2,1:T(8,128)S(1)}) conditional(s32[]{:T(128)} %convert_element_type.58, (s32[1,1536]{1,0:T(1,128)S(1)}, s32[384]{0:T(512)S(1)}, bf16[8,1536,1,128]{3,1,2,0:T(8,128)(2,1)}, s32[]{:T(128)}, bf16[384,1,4,128]{3,0,2,1:T(8,128)(2,1)S(1)}, ...), branch_computations={%region_3.5_spmd, %region_6.6_spmd} | conditional | flops 1227821568 | bytes 33530396 | solution.py:89
  232.2 2.5 fusion
  234.7 1.7 fusion.4
  236.4 3.2 %fusion.12 = f32[384,1,4,128]{0,3,2,1:T(8,128)S(1)} fusion(f32[1536,384,4]{1,0,2:T(8,128)S(1)} %get-tuple-element.191, f32[4,384]{1,0:T(4,128)S(1)} %bitcast.95, pred[384,1536]{0,1:T(8,128)(4,1)S(1)} %broadcast_compare_fusion, f32[384,1,4,128]{0,3,2,1:T(8,128)S(1)} %get-tuple-element.124, bf16[8,1536,1,128]{1,3,2,0:T(8,128)(2,1)} %get-tuple-element.125, ...), kind=kOutput, calls=%fused_computation.12 | convolution fusion | flops 611450880 | bytes 12005888 | tf_op jit(solution)/shard_map/while/body/eval_jaxpr/cond/branch_0_fun/hgrk,khd->rhgd/dot_general | solution.py:43
  239.6 0.7 fusion.46
  241.5 7.9 %conditional.2 = (f32[1,4,384]{2,1,0:T(4,128)S(1)}, f32[1,4,384]{2,1,0:T(4,128)S(1)}, f32[384,1,4,128]{0,3,2,1:T(8,128)S(1)}) conditional(s32[]{:T(128)} %convert_element_type.58, (s32[1,1536]{1,0:T(1,128)S(1)}, s32[384]{0:T(512)S(1)}, bf16[8,1536,1,128]{3,1,2,0:T(8,128)(2,1)}, s32[]{:T(128)}, bf16[384,1,4,128]{3,0,2,1:T(8,128)(2,1)S(1)}, ...), branch_computations={%region_3.5_spmd, %region_6.6_spmd} | conditional | flops 1227821568 | bytes 33530396 | solution.py:89
  242.0 2.5 fusion
  244.5 1.7 fusion.4
  246.2 3.2 %fusion.12 = f32[384,1,4,128]{0,3,2,1:T(8,128)S(1)} fusion(f32[1536,384,4]{1,0,2:T(8,128)S(1)} %get-tuple-element.191, f32[4,384]{1,0:T(4,128)S(1)} %bitcast.95, pred[384,1536]{0,1:T(8,128)(4,1)S(1)} %broadcast_compare_fusion, f32[384,1,4,128]{0,3,2,1:T(8,128)S(1)} %get-tuple-element.124, bf16[8,1536,1,128]{1,3,2,0:T(8,128)(2,1)} %get-tuple-element.125, ...), kind=kOutput, calls=%fused_computation.12 | convolution fusion | flops 611450880 | bytes 12005888 | tf_op jit(solution)/shard_map/while/body/eval_jaxpr/cond/branch_0_fun/hgrk,khd->rhgd/dot_general | solution.py:43
  249.4 0.7 fusion.46
  251.4 7.9 %conditional.2 = (f32[1,4,384]{2,1,0:T(4,128)S(1)}, f32[1,4,384]{2,1,0:T(4,128)S(1)}, f32[384,1,4,128]{0,3,2,1:T(8,128)S(1)}) conditional(s32[]{:T(128)} %convert_element_type.58, (s32[1,1536]{1,0:T(1,128)S(1)}, s32[384]{0:T(512)S(1)}, bf16[8,1536,1,128]{3,1,2,0:T(8,128)(2,1)}, s32[]{:T(128)}, bf16[384,1,4,128]{3,0,2,1:T(8,128)(2,1)S(1)}, ...), branch_computations={%region_3.5_spmd, %region_6.6_spmd} | conditional | flops 1227821568 | bytes 33530396 | solution.py:89
  251.8 2.5 fusion
  254.3 1.7 fusion.4
  256.0 3.2 %fusion.12 = f32[384,1,4,128]{0,3,2,1:T(8,128)S(1)} fusion(f32[1536,384,4]{1,0,2:T(8,128)S(1)} %get-tuple-element.191, f32[4,384]{1,0:T(4,128)S(1)} %bitcast.95, pred[384,1536]{0,1:T(8,128)(4,1)S(1)} %broadcast_compare_fusion, f32[384,1,4,128]{0,3,2,1:T(8,128)S(1)} %get-tuple-element.124, bf16[8,1536,1,128]{1,3,2,0:T(8,128)(2,1)} %get-tuple-element.125, ...), kind=kOutput, calls=%fused_computation.12 | convolution fusion | flops 611450880 | bytes 12005888 | tf_op jit(solution)/shard_map/while/body/eval_jaxpr/cond/branch_0_fun/hgrk,khd->rhgd/dot_general | solution.py:43
  259.2 0.7 fusion.46
  261.2 7.9 %conditional.2 = (f32[1,4,384]{2,1,0:T(4,128)S(1)}, f32[1,4,384]{2,1,0:T(4,128)S(1)}, f32[384,1,4,128]{0,3,2,1:T(8,128)S(1)}) conditional(s32[]{:T(128)} %convert_element_type.58, (s32[1,1536]{1,0:T(1,128)S(1)}, s32[384]{0:T(512)S(1)}, bf16[8,1536,1,128]{3,1,2,0:T(8,128)(2,1)}, s32[]{:T(128)}, bf16[384,1,4,128]{3,0,2,1:T(8,128)(2,1)S(1)}, ...), branch_computations={%region_3.5_spmd, %region_6.6_spmd} | conditional | flops 1227821568 | bytes 33530396 | solution.py:89
  261.6 2.5 fusion
  264.1 1.7 fusion.4
  265.9 3.2 %fusion.12 = f32[384,1,4,128]{0,3,2,1:T(8,128)S(1)} fusion(f32[1536,384,4]{1,0,2:T(8,128)S(1)} %get-tuple-element.191, f32[4,384]{1,0:T(4,128)S(1)} %bitcast.95, pred[384,1536]{0,1:T(8,128)(4,1)S(1)} %broadcast_compare_fusion, f32[384,1,4,128]{0,3,2,1:T(8,128)S(1)} %get-tuple-element.124, bf16[8,1536,1,128]{1,3,2,0:T(8,128)(2,1)} %get-tuple-element.125, ...), kind=kOutput, calls=%fused_computation.12 | convolution fusion | flops 611450880 | bytes 12005888 | tf_op jit(solution)/shard_map/while/body/eval_jaxpr/cond/branch_0_fun/hgrk,khd->rhgd/dot_general | solution.py:43
  269.1 0.7 fusion.46
  271.0 7.9 %conditional.2 = (f32[1,4,384]{2,1,0:T(4,128)S(1)}, f32[1,4,384]{2,1,0:T(4,128)S(1)}, f32[384,1,4,128]{0,3,2,1:T(8,128)S(1)}) conditional(s32[]{:T(128)} %convert_element_type.58, (s32[1,1536]{1,0:T(1,128)S(1)}, s32[384]{0:T(512)S(1)}, bf16[8,1536,1,128]{3,1,2,0:T(8,128)(2,1)}, s32[]{:T(128)}, bf16[384,1,4,128]{3,0,2,1:T(8,128)(2,1)S(1)}, ...), branch_computations={%region_3.5_spmd, %region_6.6_spmd} | conditional | flops 1227821568 | bytes 33530396 | solution.py:89
  271.0 0.4 broadcast_compare_fusion
  271.4 2.5 fusion
  274.0 1.7 fusion.4
  275.7 3.2 %fusion.12 = f32[384,1,4,128]{0,3,2,1:T(8,128)S(1)} fusion(f32[1536,384,4]{1,0,2:T(8,128)S(1)} %get-tuple-element.191, f32[4,384]{1,0:T(4,128)S(1)} %bitcast.95, pred[384,1536]{0,1:T(8,128)(4,1)S(1)} %broadcast_compare_fusion, f32[384,1,4,128]{0,3,2,1:T(8,128)S(1)} %get-tuple-element.124, bf16[8,1536,1,128]{1,3,2,0:T(8,128)(2,1)} %get-tuple-element.125, ...), kind=kOutput, calls=%fused_computation.12 | convolution fusion | flops 611450880 | bytes 12005888 | tf_op jit(solution)/shard_map/while/body/eval_jaxpr/cond/branch_0_fun/hgrk,khd->rhgd/dot_general | solution.py:43
  279.0 0.9 copy.23
  (70 shorter events, 4.2 us)
Async XLA Ops:
  6.5 1.6 copy-start
  6.5 143.1 %all-gather.7.cloned.1.call-start = ((), (), s32[]{:S(2)}) async-start(), calls=%async_computation.2 | async-start | bytes 3244032 | tf_op jit(solution)/shard_map/all_gather | solution.py:135
  90.8 1.7 copy-start.1
  90.8 3.4 %copy-start.3 = (bf16[4096,128]{1,0:T(8,128)(2,1)S(1)}, bf16[4096,128]{1,0:T(8,128)(2,1)}, u32[]{:S(2)}) copy-start(bf16[4096,128]{1,0:T(8,128)(2,1)} %param.15) | copy-start | bytes 3145732
  92.5 1.6 copy-start.2
  92.5 3.4 %copy-start.4 = (bf16[4096,128]{1,0:T(8,128)(2,1)S(1)}, bf16[4096,128]{1,0:T(8,128)(2,1)}, u32[]{:S(2)}) copy-start(bf16[4096,128]{1,0:T(8,128)(2,1)} %param.14) | copy-start | bytes 3145732
  95.8 99.8 %all-gather.5.cloned.1.call-start = ((), (), s32[]{:S(2)}) async-start(), calls=%async_computation.1 | async-start | bytes 3244032 | tf_op jit(solution)/shard_map/all_gather | solution.py:134
  99.9 32.1 %copy-start.5 = (s32[384]{0:T(512)S(1)}, s32[384]{0:T(512)}, u32[]{:S(2)}) copy-start(s32[384]{0:T(512)} %param.11) | copy-start | bytes 4612
  99.9 32.1 %copy-start.6 = (f32[384]{0:T(512)S(1)}, f32[384]{0:T(512)}, u32[]{:S(2)}) copy-start(f32[384]{0:T(512)} %param.12) | copy-start | bytes 4612
Sparse Core Ops, SparseCore 0:
  95.9 46.1 all-gather.6
  144.5 51.0 all-gather.4
